TPU v7x, 256 devices: a whole 4x4x8 slice. The times are simulated.
256 devices in a mesh: seq: 64 (over x, z_lo, y, core), mp: 4 (over z_hi).
Axes of the slice: x: 4, y: 4, z: 8 (z_hi: 4, z_lo: 2; z = z_hi * 2 + z_lo), core: 2. Of those that a mesh axis runs over, the one named last changes fastest.
Arguments:
- tokens: bfloat16 [8192, 4096], P('seq', 'mp'), may hold values from -6 to 6
- w_proj: bfloat16 [4096, 3, 2048], P('seq', None, 'mp'), may hold values from -0.09375 to 0.09375
- short_filter: float32 [3, 3, 2048], P(None, None, 'mp'), may hold values from -3.5 to 3.5
- long_filter: float32 [2048, 8192], P(('mp', 'seq')), may hold values from -0.0625 to 0.0625
- skip_gain: float32 [2048], P('mp'), may hold values from -4 to 4
Outputs:
- gated: bfloat16 [8192, 2048], P('seq', 'mp')
All inputs are finite; a program needn't handle non-finite values.
Results may differ from a plain program's by a relative error of at most 0.012.
Values may be sent and summed in bfloat16 or wider, within the bound.
No kernel may reach another device: no remote copies, remote signals or barrier semaphores. Data moves between devices by JAX's collectives and lax.ppermute only.
A program may use at most 64 MiB of HBM per device.

v0:
```python
import numpy as np

import jax
import jax.numpy as jnp
from jax import lax
from jax.sharding import PartitionSpec as P


PRECISION = lax.Precision.HIGH
GROUP = 8


def shifted(value, axis, steps):
    count = lax.axis_size(axis)
    leading, last = (max(0, -steps), min(count, count - steps))
    return lax.ppermute(value, axis, [(source, source + steps) for source in range(leading, last)])


def tables(rows, cols):
    first = np.arange(rows)
    second = np.arange(cols)
    outer = 2.0 * np.pi * np.outer(first, first) / rows
    inner = 2.0 * np.pi * np.outer(second, second) / cols
    twist = 2.0 * np.pi * np.outer(first, second) / (rows * cols)
    f32 = lambda a: jnp.asarray(a.astype(np.float32))
    return dict(
        outer_cos=f32(np.cos(outer)),
        outer_sin=f32(np.sin(outer)),
        inner_cos=f32(np.cos(inner)),
        inner_sin=f32(np.sin(inner)),
        twist_cos=f32(np.cos(twist)),
        twist_sin=f32(np.sin(twist)),
    )


def block(cos, sin, sign):
    return jnp.concatenate(
        [jnp.concatenate([cos, sign * sin], axis=1), jnp.concatenate([-sign * sin, cos], axis=1)], axis=0
    )


def forward(first, t, cols):
    tc = t["twist_cos"][:, None, :]
    ts = t["twist_sin"][:, None, :]
    first_re, first_im = first[..., :cols], first[..., cols:]
    turned = jnp.concatenate([first_re * tc + first_im * ts, first_im * tc - first_re * ts], axis=-1)
    matrix = block(t["inner_cos"], t["inner_sin"], -1.0)
    return jnp.einsum("krn,nm->krm", turned, matrix, precision=PRECISION)


def long_conv(signal, kernel):
    live, channels, cols = signal.shape
    rows = 2 * live
    t = lax.optimization_barrier(tables(rows, cols))
    first = jnp.concatenate([t["outer_cos"][:, :live], -t["outer_sin"][:, :live]], axis=0)
    own_kernel, own_first, own_t = lax.optimization_barrier((kernel, first, t))
    ker = jnp.einsum("kn,rnm->krm", own_first, own_kernel.reshape(channels, live, cols), precision=PRECISION)
    ker = jnp.concatenate([ker[:rows], ker[rows:]], axis=-1)
    sh = forward(ker, own_t, cols)
    sig = jnp.einsum("kn,nrm->krm", first, signal.astype(jnp.float32), precision=PRECISION)
    sig = jnp.concatenate([sig[:rows], sig[rows:]], axis=-1)
    su = forward(sig, t, cols)
    su_re, su_im = su[..., :cols], su[..., cols:]
    sh_re, sh_im = sh[..., :cols], sh[..., cols:]
    z = jnp.concatenate([su_re * sh_re - su_im * sh_im, su_re * sh_im + su_im * sh_re], axis=-1)
    d = jnp.einsum("krn,nm->krm", z, block(t["inner_cos"], t["inner_sin"], 1.0), precision=PRECISION)
    d_re, d_im = d[..., :cols], d[..., cols:]
    tc = t["twist_cos"][:, None, :]
    ts = t["twist_sin"][:, None, :]
    e = jnp.concatenate([d_re * tc - d_im * ts, d_im * tc + d_re * ts], axis=0)
    scale = 1.0 / (rows * cols)
    back = jnp.concatenate([t["outer_cos"][:live], -t["outer_sin"][:live]], axis=1) * scale
    return jnp.einsum("nk,krm->nrm", back, e, precision=PRECISION)


def pick(values, axis, parity):
    shape = values.shape
    grouped = values.reshape(shape[:axis] + (shape[axis] // (2 * GROUP), 2, GROUP) + shape[axis + 1 :])
    taken = lax.dynamic_index_in_dim(grouped, parity, axis + 1, keepdims=False)
    return taken.reshape(shape[:axis] + (shape[axis] // 2,) + shape[axis + 1 :])


def layer(tokens, w_proj, short_filter, long_filter, skip_gain):
    rows_dev = tokens.shape[0]
    margin = short_filter.shape[1] - 1
    width = w_proj.shape[2]
    half = width // 2
    chips = lax.axis_size("chip")
    parity = lax.axis_index("core")
    split = w_proj.reshape(w_proj.shape[0], 3, width // (2 * GROUP), 2, GROUP)
    split = jnp.transpose(split, (3, 0, 1, 2, 4)).reshape(1, 2, w_proj.shape[0], 3 * half)
    spread = jnp.broadcast_to(split, (chips,) + split.shape[1:]).reshape((2 * chips,) + split.shape[2:])
    arrived = lax.all_to_all(spread, ("chip", "core"), split_axis=0, concat_axis=0, tiled=True)
    weights = arrived.reshape(2 * chips * w_proj.shape[0], 3 * half)
    stacked = lax.all_gather(tokens, ("core", "mp"), axis=0, tiled=False)
    rows = 2 * rows_dev
    source = jnp.transpose(stacked.reshape(2, -1, rows_dev, tokens.shape[1]), (0, 2, 1, 3)).reshape(rows, -1)
    tail = shifted(source[rows - margin :], "chip", 1)
    extended_tokens = jnp.concatenate([tail, source], axis=0)
    taps = pick(short_filter, 2, parity)
    mixed = []
    projected_all = jnp.dot(extended_tokens, weights, preferred_element_type=jnp.float32)
    for member in range(3):
        projected = projected_all[:, member * half : (member + 1) * half]
        extended = projected.astype(jnp.bfloat16).astype(jnp.float32)
        total = jnp.zeros((rows, half), jnp.float32)
        for offset in range(margin + 1):
            total = total + taps[member, offset][None] * extended[margin - offset : margin - offset + rows]
        mixed.append(total)
    query_rows = mixed[0]
    product = (mixed[1] * mixed[2]).astype(jnp.bfloat16)
    outgoing = product.T.reshape(chips, GROUP, rows)
    arrived = lax.all_to_all(outgoing, "chip", split_axis=0, concat_axis=0, tiled=True)
    convolved = long_conv(arrived, long_filter).astype(jnp.bfloat16)
    mine = lambda values: lax.dynamic_slice_in_dim(values, parity * rows_dev, rows_dev, axis=0)
    theirs = lambda values: lax.dynamic_slice_in_dim(values, (1 - parity) * rows_dev, rows_dev, axis=0)
    pairs = [(0, 1), (1, 0)]
    query_other = lax.ppermute(theirs(query_rows), "core", pairs)
    product_other = lax.ppermute(theirs(product), "core", pairs)

    def whole(own, other):
        first = jnp.where(parity == 0, own, other)
        second = jnp.where(parity == 0, other, own)
        both = jnp.stack([first, second]).reshape(2, rows_dev, half // GROUP, GROUP)
        return jnp.transpose(both, (1, 2, 0, 3)).reshape(rows_dev, width)

    query_full = whole(mine(query_rows), query_other)
    product_full = whole(mine(product), product_other).astype(jnp.float32)
    outgoing = convolved.reshape(chips, GROUP, 2, rows_dev).transpose(0, 2, 1, 3).reshape(2 * chips, GROUP, rows_dev)
    returned = lax.all_to_all(outgoing, ("chip", "core"), split_axis=0, concat_axis=0, tiled=True)
    back_rows = returned.reshape(width, rows_dev).T
    result = query_full * (back_rows.astype(jnp.float32) + skip_gain[None, :] * product_full)
    return result.astype(jnp.bfloat16)


def solution(mesh):
    seq_size = mesh.shape["seq"]
    devices = mesh.devices.reshape(seq_size // 2, 2, mesh.shape["mp"])
    inner = jax.sharding.Mesh(devices, ("chip", "core", "mp"))
    seq = ("chip", "core")
    return jax.shard_map(
        layer,
        mesh=inner,
        in_specs=(
            P(seq, "mp"),
            P(seq, None, "mp"),
            P(None, None, "mp"),
            P(("mp",) + seq, None),
            P("mp"),
        ),
        out_specs=P(seq, "mp"),
        check_vma=False,
    )
```

profile of v0, /device:TPU:1, one launch (start us, length us, event | category | flops | bytes accessed | tf_op | source)
XLA Modules:
  0.0 160.3 jit_solution(12858227341484379400)
XLA Ops:
  6.5 1.2 copy.84
  7.8 0.2 copy.86
  8.0 3.4 %broadcast_in_dim.5 = bf16[32,2,64,768]{3,2,1,0:T(8,128)(2,1)} broadcast(bf16[2,64,768]{2,1,0:T(8,128)(2,1)S(1)} %copy.86), dimensions={1,2,3} | broadcast | bytes 6488064 | tf_op jit(solution)/shard_map/broadcast_in_dim | solution.py:92
  11.4 10.6 %all-to-all-start = ((bf16[64,64,768]{2,1,0:T(8,128)(2,1)}), bf16[64,64,768]{2,1,0:T(8,128)(2,1)}, u32[]{:S(2)}, u32[]{:S(2)}) async-start(bf16[64,64,768]{2,1,0:T(8,128)(2,1)} %bitcast.72), calls=%async_computation | async-start | bytes 12582912 | tf_op jit(solution)/shard_map/all_to_all | solution.py:93
  22.1 0.7 all-gather.3.cloned.1.call-update
  22.8 0.5 reshape.67
  23.3 0.4 dynamic-slice_reduce_fusion
  23.7 0.1 reshape.68
  23.9 0.1 copy.90
  24.0 0.1 pad_maximum_fusion.10
  24.1 0.6 fusion.43
  24.8 0.1 multiply_add_fusion.2
  24.9 0.1 pad_maximum_fusion.7
  25.0 0.6 copy-done.1
  25.8 1.5 fusion.17
  27.2 45.0 %all-gather.3.cloned.1.call-done = bf16[1024,1024]{1,0:T(8,128)(2,1)} async-done(((bf16[128,1024]{1,0:T(8,128)(2,1)}), bf16[1024,1024]{1,0:T(8,128)(2,1)}) %all-gather.3.cloned.1.call-update) | async-done | bytes 2097168 | tf_op jit(solution)/shard_map/all_gather | solution.py:95
  72.2 3.2 %copy.83 = bf16[2,4,128,1024]{3,1,2,0:T(4,128)(2,1)S(1)} copy(bf16[2,4,128,1024]{3,2,1,0:T(8,128)(2,1)} %bitcast.76) | data formatting | bytes 4194304 | tf_op jit(solution)/shard_map/reshape | solution.py:97
  75.4 0.9 copy.106
  76.3 1.3 copy-done.3
  77.6 2.1 %collective-permute-start = (bf16[2,4096]{1,0:T(2,128)(2,1)S(1)}, bf16[2,4096]{1,0:T(2,128)(2,1)S(1)}, u32[]{:S(2)}, u32[]{:S(2)}) collective-permute-start(bf16[2,4096]{1,0:T(2,128)(2,1)S(1)} %slice.156), channel_id=1, source_target_pairs={{0,8},{8,16},{16,24},{24,32},{32,40},{40,48},{48,56},{56,64},{64,7... | collective-permute-start | bytes 49160 | tf_op jit(solution)/shard_map/ppermute | solution.py:16
  79.8 0.8 collective-permute-done
  80.6 33.0 %all-to-all-done = bf16[64,64,768]{2,1,0:T(8,128)(2,1)} async-done(((bf16[64,64,768]{2,1,0:T(8,128)(2,1)}), bf16[64,64,768]{2,1,0:T(8,128)(2,1)}, u32[]{:S(2)}, u32[]{:S(2)}) %all-to-all-start) | async-done | bytes 6291488 | tf_op jit(solution)/shard_map/all_to_all | solution.py:93
  113.6 5.3 %fusion.4 = bf16[258,768]{1,0:T(8,128)(2,1)S(1)} fusion(bf16[4096,768]{1,0:T(8,128)(2,1)} %bitcast.7, bf16[256,4096]{1,0:T(8,128)(2,1)} %bitcast.75, bf16[2,4096]{1,0:T(2,128)(2,1)S(1)} %collective-permute-done), kind=kOutput, calls=%fused_computation.8 | convolution fusion | flops 1627620864 | bytes 8801280 | tf_op jit(solution)/shard_map/dot_general | solution.py:102
  118.9 0.2 fusion.34
  119.1 0.1 collective-permute-start.2
  119.2 0.1 fusion.38
  119.4 0.6 collective-permute-start.1
  119.9 0.8 copy.92
  120.7 4.5 %all-to-all-start.1 = ((bf16[32,8,256]{2,1,0:T(8,128)(2,1)}), bf16[32,8,256]{2,1,0:T(8,128)(2,1)S(1)}, u32[]{:S(2)}, u32[]{:S(2)}) async-start(bf16[32,8,256]{2,1,0:T(8,128)(2,1)} %bitcast.23), calls=%async_computation.1 | async-start | bytes 262144 | tf_op jit(solution)/shard_map/all_to_all | solution.py:113
  125.2 0.1 copy.101
  125.3 0.1 copy.100
  125.5 7.0 %all-to-all-done.1 = bf16[32,8,256]{2,1,0:T(8,128)(2,1)S(1)} async-done(((bf16[32,8,256]{2,1,0:T(8,128)(2,1)}), bf16[32,8,256]{2,1,0:T(8,128)(2,1)S(1)}, u32[]{:S(2)}, u32[]{:S(2)}) %all-to-all-start.1) | async-done | bytes 131104 | tf_op jit(solution)/shard_map/all_to_all | solution.py:113
  132.6 0.5 fusion.45
  133.0 0.1 multiply_add_fusion.3
  133.2 0.1 pad_maximum_fusion.6
  133.3 1.5 fusion.9
  134.8 0.1 multiply_subtract_fusion.1
  134.9 0.1 pad_maximum_fusion.8
  135.1 1.5 fusion.13
  136.6 0.1 multiply_subtract_fusion
  136.7 0.4 convolution_convert_fusion
  137.2 0.7 copy.99
  137.9 6.0 %all-to-all-start.2 = ((bf16[64,8,128]{2,1,0:T(8,128)(2,1)}), bf16[64,8,128]{2,1,0:T(8,128)(2,1)S(1)}, u32[]{:S(2)}, u32[]{:S(2)}) async-start(bf16[64,8,128]{2,1,0:T(8,128)(2,1)} %bitcast.29), calls=%async_computation.2 | async-start | bytes 262144 | tf_op jit(solution)/shard_map/all_to_all | solution.py:130
  143.9 0.1 copy.88
  144.0 0.1 copy.87
  144.2 8.3 %all-to-all-done.2 = bf16[64,8,128]{2,1,0:T(8,128)(2,1)S(1)} async-done(((bf16[64,8,128]{2,1,0:T(8,128)(2,1)}), bf16[64,8,128]{2,1,0:T(8,128)(2,1)S(1)}, u32[]{:S(2)}, u32[]{:S(2)}) %all-to-all-start.2) | async-done | bytes 131104 | tf_op jit(solution)/shard_map/all_to_all | solution.py:130
  152.5 0.1 fusion.42
  152.6 0.8 copy.103
  (41 shorter events, 0.6 us)
Async XLA Ops:
  6.5 17.5 %copy-start = (f32[8,8192]{1,0:T(8,128)S(1)}, f32[8,8192]{1,0:T(8,128)}, u32[]{:S(2)}) copy-start(f32[8,8192]{1,0:T(8,128)} %param.14) | copy-start | bytes 786436
  11.4 11.4 %copy-start.8 = (f32[3,3,512]{2,1,0:T(4,128)S(1)}, f32[3,3,512]{2,1,0:T(4,128)}, u32[]{:S(2)}) copy-start(f32[3,3,512]{2,1,0:T(4,128)} %param.13) | copy-start | bytes 55300
  11.4 12.5 %copy-start.7 = (f32[64,64]{1,0:T(8,128)S(1)}, f32[64,64]{1,0:T(8,128)}, u32[]{:S(2)}) copy-start(f32[64,64]{1,0:T(8,128)} %constant.36.clone) | copy-start | bytes 49156
  11.4 12.6 %copy-start.6 = (f32[64,64]{1,0:T(8,128)S(1)}, f32[64,64]{1,0:T(8,128)}, u32[]{:S(2)}) copy-start(f32[64,64]{1,0:T(8,128)} %constant.35.clone) | copy-start | bytes 49156
  11.4 102.2 %all-to-all-start = ((bf16[64,64,768]{2,1,0:T(8,128)(2,1)}), bf16[64,64,768]{2,1,0:T(8,128)(2,1)}, u32[]{:S(2)}, u32[]{:S(2)}) async-start(bf16[64,64,768]{2,1,0:T(8,128)(2,1)} %bitcast.72), calls=%async_computation | async-start | bytes 12582912 | tf_op jit(solution)/shard_map/all_to_all | solution.py:93
  22.0 2.7 %copy-start.4 = (f32[64,256]{1,0:T(8,128)S(1)}, f32[64,256]{1,0:T(8,128)}, u32[]{:S(2)}) copy-start(f32[64,256]{1,0:T(8,128)} %constant.39.clone) | copy-start | bytes 196612
  22.0 2.7 %copy-start.5 = (f32[64,256]{1,0:T(8,128)S(1)}, f32[64,256]{1,0:T(8,128)}, u32[]{:S(2)}) copy-start(f32[64,256]{1,0:T(8,128)} %constant.40.clone) | copy-start | bytes 196612
  22.0 50.2 %all-gather.3.cloned.1.call-start = ((), (), s32[]{:S(2)}) async-start(), calls=%async_computation.3 | async-start | bytes 2359296 | tf_op jit(solution)/shard_map/all_gather | solution.py:95
  24.7 1.0 copy-start.1
  24.7 1.0 copy-start.2
  76.3 1.3 copy-start.3
  77.6 3.0 %collective-permute-start = (bf16[2,4096]{1,0:T(2,128)(2,1)S(1)}, bf16[2,4096]{1,0:T(2,128)(2,1)S(1)}, u32[]{:S(2)}, u32[]{:S(2)}) collective-permute-start(bf16[2,4096]{1,0:T(2,128)(2,1)S(1)} %slice.156), channel_id=1, source_target_pairs={{0,8},{8,16},{16,24},{24,32},{32,40},{40,48},{48,56},{56,64},{64,7... | collective-permute-start | bytes 49160 | tf_op jit(solution)/shard_map/ppermute | solution.py:16
  119.1 6.0 %collective-permute-start.2 = (bf16[128,256]{1,0:T(8,128)(2,1)S(1)}, bf16[128,256]{1,0:T(8,128)(2,1)S(1)}, u32[]{:S(2)}, u32[]{:S(2)}) collective-permute-start(bf16[128,256]{1,0:T(8,128)(2,1)S(1)} %constant_dynamic-slice_fusion), channel_id=1, source_target_pairs={{0,4},{4,0},{1,5},{5,1},{2,6},{6,2},{3,7},{7,3},{8,12},{12,8},{9,1... | collective-permute-start | bytes 196616 | tf_op jit(solution)/shard_map/ppermute | solution.py:119
  119.4 24.5 %collective-permute-start.1 = (f32[128,256]{1,0:T(8,128)S(1)}, f32[128,256]{1,0:T(8,128)S(1)}, u32[]{:S(2)}, u32[]{:S(2)}) collective-permute-start(f32[128,256]{1,0:T(8,128)S(1)} %constant_dynamic-slice_fusion.1), channel_id=1, source_target_pairs={{0,4},{4,0},{1,5},{5,1},{2,6},{6,2},{3,7},{7,3},{8,12},{12,8},{9,1... | collective-permute-start | bytes 393224 | tf_op jit(solution)/shard_map/ppermute | solution.py:118
  120.7 11.9 %all-to-all-start.1 = ((bf16[32,8,256]{2,1,0:T(8,128)(2,1)}), bf16[32,8,256]{2,1,0:T(8,128)(2,1)S(1)}, u32[]{:S(2)}, u32[]{:S(2)}) async-start(bf16[32,8,256]{2,1,0:T(8,128)(2,1)} %bitcast.23), calls=%async_computation.1 | async-start | bytes 262144 | tf_op jit(solution)/shard_map/all_to_all | solution.py:113
  136.7 15.8 %copy-start.9 = (f32[512]{0:T(512)S(1)}, f32[512]{0:T(512)}, u32[]{:S(2)}) copy-start(f32[512]{0:T(512)} %param.15) | copy-start | bytes 6148
  137.9 14.6 %all-to-all-start.2 = ((bf16[64,8,128]{2,1,0:T(8,128)(2,1)}), bf16[64,8,128]{2,1,0:T(8,128)(2,1)S(1)}, u32[]{:S(2)}, u32[]{:S(2)}) async-start(bf16[64,8,128]{2,1,0:T(8,128)(2,1)} %bitcast.29), calls=%async_computation.2 | async-start | bytes 262144 | tf_op jit(solution)/shard_map/all_to_all | solution.py:130
Sparse Core Ops, SparseCore 0:
  24.7 47.4 all-gather.2
where the time goes:
time: 161 us; the launch traced here: 160 us
  waiting for transfers between devices  94.8 us (59%)
  starting transfers between devices  23.9 us (15%)
  local copies, waits for them, and re-layouts  14.8 us (9%)
  between operations  13.9 us (9%)
  matrix products  11.2 us (7%)
  other arithmetic  1.62 us (1%)
    all_gather x1, waiting for transfers between devices, layer(): stacked = lax.all_gather(tokens, ('core', 'mp'), axis=0, tiled=False)  45 us
    all_to_all x1, waiting for transfers between devices, layer(): lax.all_to_all(spread, ('chip', 'core'), split_axis=0, concat_axis=0, til...  33 us
    all_to_all x1, starting transfers between devices, layer(): lax.all_to_all(spread, ('chip', 'core'), split_axis=0, concat_axis=0, til...  10.6 us
    all_to_all x1, waiting for transfers between devices, layer(): lax.all_to_all(outgoing, ('chip', 'core'), split_axis=0, concat_axis=0, t...  8.31 us
    all_to_all x1, waiting for transfers between devices, layer(): lax.all_to_all(outgoing, 'chip', split_axis=0, concat_axis=0, tiled=True)  7.05 us
    all_to_all x1, starting transfers between devices, layer(): lax.all_to_all(outgoing, ('chip', 'core'), split_axis=0, concat_axis=0, t...  5.96 us
    dot_general x1, matrix products, layer(): jnp.dot(extended_tokens, weights, preferred_element_type=jnp.float32)  5.29 us
    all_to_all x1, starting transfers between devices, layer(): lax.all_to_all(outgoing, 'chip', split_axis=0, concat_axis=0, tiled=True)  4.46 us
  transfers between devices with their start and end apart: 7, of which 5 were waited for; matrix products, arithmetic and copies ran while one was open for 9% of the time, Pallas kernels for 0%

commit v1 on v0

--- a/solution.py
+++ b/solution.py
@@ -98,17 +98,22 @@
     tail = shifted(source[rows - margin :], "chip", 1)
     extended_tokens = jnp.concatenate([tail, source], axis=0)
     taps = pick(short_filter, 2, parity)
-    mixed = []
-    projected_all = jnp.dot(extended_tokens, weights, preferred_element_type=jnp.float32)
-    for member in range(3):
-        projected = projected_all[:, member * half : (member + 1) * half]
-        extended = projected.astype(jnp.bfloat16).astype(jnp.float32)
-        total = jnp.zeros((rows, half), jnp.float32)
-        for offset in range(margin + 1):
-            total = total + taps[member, offset][None] * extended[margin - offset : margin - offset + rows]
-        mixed.append(total)
-    query_rows = mixed[0]
-    product = (mixed[1] * mixed[2]).astype(jnp.bfloat16)
+
+    def branches(columns, members):
+        projected_all = jnp.dot(extended_tokens, columns, preferred_element_type=jnp.float32)
+        mixed = []
+        for index, member in enumerate(members):
+            projected = projected_all[:, index * half : (index + 1) * half]
+            extended = projected.astype(jnp.bfloat16).astype(jnp.float32)
+            total = jnp.zeros((rows, half), jnp.float32)
+            for offset in range(margin + 1):
+                total = total + taps[member, offset][None] * extended[margin - offset : margin - offset + rows]
+            mixed.append(total)
+        return mixed
+
+    key_rows, value_rows = branches(weights[:, half:], (1, 2))
+    product = (key_rows * value_rows).astype(jnp.bfloat16)
+    (query_rows,) = branches(weights[:, :half], (0,))
     outgoing = product.T.reshape(chips, GROUP, rows)
     arrived = lax.all_to_all(outgoing, "chip", split_axis=0, concat_axis=0, tiled=True)
     convolved = long_conv(arrived, long_filter).astype(jnp.bfloat16)

time: 161 us -> 163 us (1.012)
    unnamed x22 -> x24, local copies, waits for them, and re-layouts: 4.06 us -> 5.29 us
    dot_general x1 -> x2, matrix products: 5.29 us -> 6.48 us  [branches(): jnp.dot(extended_tokens, columns, preferred_element_type=jnp.float32)]
  transfers between devices with their start and end apart: 7 -> 7, of which waited for: 5 -> 5; matrix products, arithmetic and copies ran while one was open for 9% -> 10% of each run, Pallas kernels for 0% -> 0%
where the time goes in v1:
time: 163 us; the launch traced here: 162 us
  waiting for transfers between devices  94.8 us (58%)
  starting transfers between devices  23.4 us (14%)
  local copies, waits for them, and re-layouts  16 us (10%)
  between operations  13.9 us (9%)
  matrix products  12.4 us (8%)
    all_gather x1, waiting for transfers between devices, layer(): stacked = lax.all_gather(tokens, ('core', 'mp'), axis=0, tiled=False)  45 us
    all_to_all x1, waiting for transfers between devices, layer(): lax.all_to_all(spread, ('chip', 'core'), split_axis=0, concat_axis=0, til...  33 us
    all_to_all x1, starting transfers between devices, layer(): lax.all_to_all(spread, ('chip', 'core'), split_axis=0, concat_axis=0, til...  10.6 us
    all_to_all x1, waiting for transfers between devices, layer(): lax.all_to_all(outgoing, ('chip', 'core'), split_axis=0, concat_axis=0, t...  8.31 us
    all_to_all x1, waiting for transfers between devices, layer(): lax.all_to_all(outgoing, 'chip', split_axis=0, concat_axis=0, tiled=True)  7.04 us
    dot_general x2, matrix products, branches(): jnp.dot(extended_tokens, columns, preferred_element_type=jnp.float32)  6.48 us
    all_to_all x1, starting transfers between devices, layer(): lax.all_to_all(outgoing, ('chip', 'core'), split_axis=0, concat_axis=0, t...  5.49 us
    unnamed x24, local copies, waits for them, and re-layouts  5.29 us
  transfers between devices with their start and end apart: 7, of which 5 were waited for; matrix products, arithmetic and copies ran while one was open for 10% of the time, Pallas kernels for 0%

profile of v1, /device:TPU:1, one launch (start us, length us, event | category | flops | bytes accessed | tf_op | source)
XLA Modules:
  0.0 162.2 jit_solution(17998993433143864773)
XLA Ops:
  6.5 1.2 copy.84
  7.8 0.2 copy.86
  8.0 3.4 %broadcast_in_dim.5 = bf16[32,2,64,768]{3,2,1,0:T(8,128)(2,1)} broadcast(bf16[2,64,768]{2,1,0:T(8,128)(2,1)S(1)} %copy.86), dimensions={1,2,3} | broadcast | bytes 6488064 | tf_op jit(solution)/shard_map/broadcast_in_dim | solution.py:92
  11.4 10.6 %all-to-all-start = ((bf16[64,64,768]{2,1,0:T(8,128)(2,1)}), bf16[64,64,768]{2,1,0:T(8,128)(2,1)}, u32[]{:S(2)}, u32[]{:S(2)}) async-start(bf16[64,64,768]{2,1,0:T(8,128)(2,1)} %bitcast.71), calls=%async_computation | async-start | bytes 12582912 | tf_op jit(solution)/shard_map/all_to_all | solution.py:93
  22.1 0.7 all-gather.3.cloned.1.call-update
  22.8 0.5 reshape.67
  23.3 0.4 dynamic-slice_reduce_fusion
  23.7 0.1 reshape.68
  24.0 0.1 pad_maximum_fusion.19
  24.1 0.6 fusion.49
  24.7 0.1 multiply_add_fusion.2
  24.9 0.1 pad_maximum_fusion.16
  25.0 0.6 copy-done.1
  25.8 1.5 fusion.23
  27.2 45.0 %all-gather.3.cloned.1.call-done = bf16[1024,1024]{1,0:T(8,128)(2,1)} async-done(((bf16[128,1024]{1,0:T(8,128)(2,1)}), bf16[1024,1024]{1,0:T(8,128)(2,1)}) %all-gather.3.cloned.1.call-update) | async-done | bytes 2097168 | tf_op jit(solution)/shard_map/all_gather | solution.py:95
  72.2 3.2 %copy.83 = bf16[2,4,128,1024]{3,1,2,0:T(4,128)(2,1)S(1)} copy(bf16[2,4,128,1024]{3,2,1,0:T(8,128)(2,1)} %bitcast.76) | data formatting | bytes 4194304 | tf_op jit(solution)/shard_map/reshape | solution.py:97
  75.4 0.9 copy.106
  76.3 1.3 copy-done.3
  77.6 2.1 %collective-permute-start = (bf16[2,4096]{1,0:T(2,128)(2,1)S(1)}, bf16[2,4096]{1,0:T(2,128)(2,1)S(1)}, u32[]{:S(2)}, u32[]{:S(2)}) collective-permute-start(bf16[2,4096]{1,0:T(2,128)(2,1)S(1)} %slice.159), channel_id=1, source_target_pairs={{0,8},{8,16},{16,24},{24,32},{32,40},{40,48},{48,56},{56,64},{64,7... | collective-permute-start | bytes 49160 | tf_op jit(solution)/shard_map/ppermute | solution.py:16
  79.8 0.8 collective-permute-done
  80.6 33.0 %all-to-all-done = bf16[64,64,768]{2,1,0:T(8,128)(2,1)} async-done(((bf16[64,64,768]{2,1,0:T(8,128)(2,1)}), bf16[64,64,768]{2,1,0:T(8,128)(2,1)}, u32[]{:S(2)}, u32[]{:S(2)}) %all-to-all-start) | async-done | bytes 6291488 | tf_op jit(solution)/shard_map/all_to_all | solution.py:93
  113.6 4.1 %fusion.4 = bf16[258,512]{1,0:T(8,128)(2,1)S(1)} fusion(bf16[4096,768]{1,0:T(8,128)(2,1)} %bitcast.7, bf16[256,4096]{1,0:T(8,128)(2,1)} %bitcast.74, bf16[2,4096]{1,0:T(2,128)(2,1)S(1)} %collective-permute-done), kind=kOutput, calls=%fused_computation.9 | convolution fusion | flops 1086489600 | bytes 6572032 | tf_op jit(solution)/shard_map/dot_general | solution.py:103
  117.7 0.2 fusion.40
  117.9 0.1 collective-permute-start.2
  118.0 1.2 copy-done.4
  119.3 2.4 %fusion.10 = f32[258,256]{1,0:T(8,128)S(1)} fusion(bf16[4096,768]{1,0:T(8,128)(2,1)} %bitcast.7, bf16[256,4096]{1,0:T(8,128)(2,1)S(1)} %bitcast.75, bf16[2,4096]{1,0:T(2,128)(2,1)S(1)} %collective-permute-done), kind=kOutput, calls=%fused_computation.11 | convolution fusion | flops 545424384 | bytes 4474880 | tf_op jit(solution)/shard_map/dot_general | solution.py:103
  121.8 0.1 collective-permute-start.1
  121.9 0.8 copy.92
  122.6 4.9 %all-to-all-start.1 = ((bf16[32,8,256]{2,1,0:T(8,128)(2,1)}), bf16[32,8,256]{2,1,0:T(8,128)(2,1)S(1)}, u32[]{:S(2)}, u32[]{:S(2)}) async-start(bf16[32,8,256]{2,1,0:T(8,128)(2,1)} %bitcast.23), calls=%async_computation.1 | async-start | bytes 262144 | tf_op jit(solution)/shard_map/all_to_all | solution.py:118
  127.6 0.1 copy.101
  127.7 0.1 copy.100
  127.9 7.0 %all-to-all-done.1 = bf16[32,8,256]{2,1,0:T(8,128)(2,1)S(1)} async-done(((bf16[32,8,256]{2,1,0:T(8,128)(2,1)}), bf16[32,8,256]{2,1,0:T(8,128)(2,1)S(1)}, u32[]{:S(2)}, u32[]{:S(2)}) %all-to-all-start.1) | async-done | bytes 131104 | tf_op jit(solution)/shard_map/all_to_all | solution.py:118
  135.0 0.5 fusion.51
  135.4 0.1 multiply_add_fusion.3
  135.6 0.1 pad_maximum_fusion.15
  135.7 1.5 fusion.15
  137.2 0.1 multiply_subtract_fusion.1
  137.4 0.1 pad_maximum_fusion.17
  137.5 1.5 fusion.19
  139.0 0.1 multiply_subtract_fusion
  139.1 0.4 convolution_convert_fusion
  139.6 0.7 copy.99
  140.3 5.5 %all-to-all-start.2 = ((bf16[64,8,128]{2,1,0:T(8,128)(2,1)}), bf16[64,8,128]{2,1,0:T(8,128)(2,1)S(1)}, u32[]{:S(2)}, u32[]{:S(2)}) async-start(bf16[64,8,128]{2,1,0:T(8,128)(2,1)} %bitcast.29), calls=%async_computation.2 | async-start | bytes 262144 | tf_op jit(solution)/shard_map/all_to_all | solution.py:135
  145.9 0.1 copy.88
  146.0 0.1 copy.87
  146.1 8.3 %all-to-all-done.2 = bf16[64,8,128]{2,1,0:T(8,128)(2,1)S(1)} async-done(((bf16[64,8,128]{2,1,0:T(8,128)(2,1)}), bf16[64,8,128]{2,1,0:T(8,128)(2,1)S(1)}, u32[]{:S(2)}, u32[]{:S(2)}) %all-to-all-start.2) | async-done | bytes 131104 | tf_op jit(solution)/shard_map/all_to_all | solution.py:135
  154.4 0.1 fusion.48
  154.6 0.8 copy.103
  (44 shorter events, 0.8 us)
Async XLA Ops:
  6.5 17.5 %copy-start = (f32[8,8192]{1,0:T(8,128)S(1)}, f32[8,8192]{1,0:T(8,128)}, u32[]{:S(2)}) copy-start(f32[8,8192]{1,0:T(8,128)} %param.14) | copy-start | bytes 786436
  11.4 11.4 %copy-start.9 = (f32[3,3,512]{2,1,0:T(4,128)S(1)}, f32[3,3,512]{2,1,0:T(4,128)}, u32[]{:S(2)}) copy-start(f32[3,3,512]{2,1,0:T(4,128)} %param.13) | copy-start | bytes 55300
  11.4 12.5 %copy-start.8 = (f32[64,64]{1,0:T(8,128)S(1)}, f32[64,64]{1,0:T(8,128)}, u32[]{:S(2)}) copy-start(f32[64,64]{1,0:T(8,128)} %constant.36.clone) | copy-start | bytes 49156
  11.4 12.6 %copy-start.7 = (f32[64,64]{1,0:T(8,128)S(1)}, f32[64,64]{1,0:T(8,128)}, u32[]{:S(2)}) copy-start(f32[64,64]{1,0:T(8,128)} %constant.35.clone) | copy-start | bytes 49156
  11.4 102.2 %all-to-all-start = ((bf16[64,64,768]{2,1,0:T(8,128)(2,1)}), bf16[64,64,768]{2,1,0:T(8,128)(2,1)}, u32[]{:S(2)}, u32[]{:S(2)}) async-start(bf16[64,64,768]{2,1,0:T(8,128)(2,1)} %bitcast.71), calls=%async_computation | async-start | bytes 12582912 | tf_op jit(solution)/shard_map/all_to_all | solution.py:93
  22.0 2.7 %copy-start.5 = (f32[64,256]{1,0:T(8,128)S(1)}, f32[64,256]{1,0:T(8,128)}, u32[]{:S(2)}) copy-start(f32[64,256]{1,0:T(8,128)} %constant.39.clone) | copy-start | bytes 196612
  22.0 2.7 %copy-start.6 = (f32[64,256]{1,0:T(8,128)S(1)}, f32[64,256]{1,0:T(8,128)}, u32[]{:S(2)}) copy-start(f32[64,256]{1,0:T(8,128)} %constant.40.clone) | copy-start | bytes 196612
  22.0 50.2 %all-gather.3.cloned.1.call-start = ((), (), s32[]{:S(2)}) async-start(), calls=%async_computation.3 | async-start | bytes 2359296 | tf_op jit(solution)/shard_map/all_gather | solution.py:95
  24.7 1.0 copy-start.1
  24.7 1.0 copy-start.2
  76.3 1.3 copy-start.3
  77.6 3.0 %collective-permute-start = (bf16[2,4096]{1,0:T(2,128)(2,1)S(1)}, bf16[2,4096]{1,0:T(2,128)(2,1)S(1)}, u32[]{:S(2)}, u32[]{:S(2)}) collective-permute-start(bf16[2,4096]{1,0:T(2,128)(2,1)S(1)} %slice.159), channel_id=1, source_target_pairs={{0,8},{8,16},{16,24},{24,32},{32,40},{40,48},{48,56},{56,64},{64,7... | collective-permute-start | bytes 49160 | tf_op jit(solution)/shard_map/ppermute | solution.py:16
  117.7 1.6 copy-start.4
  117.9 9.6 %collective-permute-start.2 = (bf16[128,256]{1,0:T(8,128)(2,1)S(1)}, bf16[128,256]{1,0:T(8,128)(2,1)S(1)}, u32[]{:S(2)}, u32[]{:S(2)}) collective-permute-start(bf16[128,256]{1,0:T(8,128)(2,1)S(1)} %constant_dynamic-slice_fusion), channel_id=1, source_target_pairs={{0,4},{4,0},{1,5},{5,1},{2,6},{6,2},{3,7},{7,3},{8,12},{12,8},{9,1... | collective-permute-start | bytes 196616 | tf_op jit(solution)/shard_map/ppermute | solution.py:124
  121.8 24.1 %collective-permute-start.1 = (f32[128,256]{1,0:T(8,128)S(1)}, f32[128,256]{1,0:T(8,128)S(1)}, u32[]{:S(2)}, u32[]{:S(2)}) collective-permute-start(f32[128,256]{1,0:T(8,128)S(1)} %constant_dynamic-slice_fusion.1), channel_id=1, source_target_pairs={{0,4},{4,0},{1,5},{5,1},{2,6},{6,2},{3,7},{7,3},{8,12},{12,8},{9,1... | collective-permute-start | bytes 393224 | tf_op jit(solution)/shard_map/ppermute | solution.py:123
  122.6 12.3 %all-to-all-start.1 = ((bf16[32,8,256]{2,1,0:T(8,128)(2,1)}), bf16[32,8,256]{2,1,0:T(8,128)(2,1)S(1)}, u32[]{:S(2)}, u32[]{:S(2)}) async-start(bf16[32,8,256]{2,1,0:T(8,128)(2,1)} %bitcast.23), calls=%async_computation.1 | async-start | bytes 262144 | tf_op jit(solution)/shard_map/all_to_all | solution.py:118
  139.1 15.3 %copy-start.10 = (f32[512]{0:T(512)S(1)}, f32[512]{0:T(512)}, u32[]{:S(2)}) copy-start(f32[512]{0:T(512)} %param.15) | copy-start | bytes 6148
  140.3 14.1 %all-to-all-start.2 = ((bf16[64,8,128]{2,1,0:T(8,128)(2,1)}), bf16[64,8,128]{2,1,0:T(8,128)(2,1)S(1)}, u32[]{:S(2)}, u32[]{:S(2)}) async-start(bf16[64,8,128]{2,1,0:T(8,128)(2,1)} %bitcast.29), calls=%async_computation.2 | async-start | bytes 262144 | tf_op jit(solution)/shard_map/all_to_all | solution.py:135
Sparse Core Ops, SparseCore 0:
  24.7 47.4 all-gather.2
